TPU v7x, 512 devices: a whole 4x8x8 slice. The times are simulated.
512 devices in a mesh: req: 128 (over z, y, core), grp: 4 (over x).
Axes of the slice: x: 4, y: 8, z: 8, core: 2. Of those that a mesh axis runs over, the one named last changes fastest.
Arguments:
- owner_slab: bfloat16 [65536, 1024], P('req'), may hold values from -6 to 6
- segment_ids: int32 [128, 512], P('req'), may hold values from 0 to 511, as said below
- head_weights: bfloat16 [1024, 16, 192], P(None, 'grp')
- merge_weights: bfloat16 [16, 64, 1024], P('grp'), may hold values from -0.1875 to 0.1875
- first_gain: float32 [1024], replicated, may hold values from 0.25 to 1.75
- first_bias: float32 [1024], replicated, may hold values from -3 to 3
- up_weights: bfloat16 [1024, 4096], P('req', 'grp'), may hold values from -0.1875 to 0.1875
- down_weights: bfloat16 [4096, 1024], P('grp', 'req'), may hold values from -0.09375 to 0.09375
- second_gain: float32 [1024], replicated, may hold values from 0.25 to 1.75
- second_bias: float32 [1024], replicated, may hold values from -3 to 3
- page_table: int32 [128, 4], P('req'), may hold values from 0 to 3, each once within a row
- row_map: int32 [128, 4, 128], P('req', 'grp'), may hold values from 0 to 127, each once within a row
Outputs:
- layer_out: bfloat16 [65536, 1024], P(('req', 'grp'))
- cache_pages: bfloat16 [512, 128, 16, 128], P('req', None, 'grp')
Inputs may be any that keep to these rules, and one draw needn't show every extreme that they name: `segment_ids`: within each slab the ids start at 0, never fall and rise by at most one from row to row; in one slab all 512 rows form a single request, and in one other slab every row is a request of its own.
All inputs are finite; a program needn't handle non-finite values.
Results may differ from a plain program's by a relative error of at most 0.0075.
Values may be sent and summed in bfloat16 or wider, within the bound.
No kernel may reach another device: no remote copies, remote signals or barrier semaphores. Data moves between devices by JAX's collectives and lax.ppermute only.
A program may use at most 64 MiB of HBM per device.

v0:
```python
import math
import jax
import jax.numpy as jnp
import numpy as np
from jax import lax
from jax.sharding import Mesh
from jax.sharding import PartitionSpec as P

EPSILON = 1e-05
REQ = ("rz", "ry", "rc")


def layer_norm(values, gain, bias):
    center = values - jnp.mean(values, axis=-1, keepdims=True)
    spread = jnp.mean(center * center, axis=-1, keepdims=True)
    return center * lax.rsqrt(spread + EPSILON) * gain + bias


def split_req(mesh):
    column = mesh.devices[:, 0]
    try:
        cores = len({d.core_on_chip for d in column})
        ys = len({d.coords[1] for d in column})
        zs = len({d.coords[2] for d in column})
    except AttributeError:
        return (column.shape[0], 1, 1)
    if zs * ys * cores != column.shape[0]:
        return (column.shape[0], 1, 1)
    return (zs, ys, cores)


def gather_rows(block, first, second):
    a = lax.all_gather(block, first, axis=0, tiled=False)
    b = lax.all_gather(a, second, axis=0, tiled=False)
    c = lax.all_gather(b, "rc", axis=0, tiled=False)
    if first == "ry":
        c = jnp.transpose(c, (1, 2, 0, 3, 4))
    else:
        c = jnp.transpose(c, (2, 1, 0, 3, 4))
    return c.reshape(-1, block.shape[1])


def local(
    owner_slab,
    segment_ids,
    head_weights,
    merge_weights,
    first_gain,
    first_bias,
    up_weights,
    down_weights,
    second_gain,
    second_bias,
    page_table,
    row_map,
):
    group = lax.axis_size("grp")
    owners = lax.axis_size(REQ)
    zs = lax.axis_size("rz")
    rows_all = owner_slab.shape[0]
    width = owner_slab.shape[1]
    quarter = rows_all // group
    local_heads = head_weights.shape[1]
    head_dim = head_weights.shape[2] // 3
    up_full = gather_rows(up_weights, "ry", "rz")
    down_full_t = gather_rows(jnp.transpose(down_weights), "rz", "ry")
    projected = jnp.einsum(
        "nd,dhc->nhc", owner_slab, head_weights, preferred_element_type=jnp.float32
    ).astype(jnp.bfloat16)
    queries = jnp.moveaxis(projected[:, :, :head_dim], 1, 0)
    key_rows = jnp.moveaxis(projected[:, :, head_dim : 2 * head_dim], 1, 0)
    value_rows = jnp.moveaxis(projected[:, :, 2 * head_dim :], 1, 0)
    segment = segment_ids[0]
    position = jnp.arange(rows_all, dtype=jnp.int32)
    allowed = (position[:, None] >= position[None, :]) & (segment[:, None] == segment[None, :])
    scale = 1.0 / math.sqrt(head_dim)

    def one_head(operands):
        query_head, key_head, value_head = operands
        scores = (
            lax.dot_general(
                query_head, key_head, (((1,), (1,)), ((), ())), preferred_element_type=jnp.float32
            )
            * scale
        )
        scores = jnp.where(allowed, scores, -1e30)
        probs = jax.nn.softmax(scores, axis=-1).astype(jnp.bfloat16)
        return jnp.dot(probs, value_head, preferred_element_type=jnp.float32).astype(jnp.bfloat16)

    attended = jnp.moveaxis(lax.map(one_head, (queries, key_rows, value_rows)), 0, 1)
    own = lax.axis_index("grp")
    own_rows = lax.dynamic_slice_in_dim(owner_slab, own * quarter, quarter, 0).astype(jnp.float32)
    partial_rows = jnp.einsum(
        "nhd,hde->ne", attended, merge_weights, preferred_element_type=jnp.float32
    )
    mixed = lax.psum_scatter(partial_rows, "grp", scatter_dimension=0, tiled=True)
    hidden = layer_norm(own_rows + mixed, first_gain, first_bias).astype(jnp.bfloat16)
    slots = quarter // owners
    placed = jnp.zeros_like(hidden).at[row_map[0, 0]].set(hidden)
    staged = placed.reshape(zs, owners // zs, slots * width)
    staged = lax.all_to_all(staged, "rz", split_axis=0, concat_axis=0, tiled=True)
    staged = lax.all_to_all(staged, ("ry", "rc"), split_axis=1, concat_axis=1, tiled=True)
    even_rows = staged.reshape(quarter, width)
    group_rows = lax.all_gather(even_rows, "grp", axis=0, tiled=True)
    raised = jnp.dot(group_rows, up_full, preferred_element_type=jnp.float32)
    activated = jax.nn.gelu(raised, approximate=False).astype(jnp.bfloat16)
    lowered_all = lax.dot_general(
        activated, down_full_t, (((1,), (1,)), ((), ())), preferred_element_type=jnp.float32
    )
    lowered = lax.psum_scatter(lowered_all, "grp", scatter_dimension=0, tiled=True)
    layer_out = layer_norm(
        even_rows.astype(jnp.float32) + lowered, second_gain, second_bias
    ).astype(jnp.bfloat16)
    page_count = page_table.shape[1]
    page_rows = rows_all // page_count
    stacked = projected[:, :, head_dim:].reshape(page_count, page_rows, local_heads, 2 * head_dim)
    cache_pages = jnp.zeros_like(stacked).at[page_table[0]].set(stacked)
    return (layer_out, cache_pages)


def solution(mesh):
    zs, ys, cores = split_req(mesh)
    devices = np.asarray(mesh.devices).reshape(zs, ys, cores, mesh.devices.shape[1])
    inner = Mesh(devices, REQ + ("grp",))
    in_specs = (
        P(REQ, None),
        P(REQ, None),
        P(None, "grp", None),
        P("grp", None, None),
        P(),
        P(),
        P(REQ, "grp"),
        P("grp", REQ),
        P(),
        P(),
        P(REQ, None),
        P(REQ, "grp", None),
    )
    out_specs = (P(REQ + ("grp",), None), P(REQ, None, "grp", None))
    return jax.shard_map(local, mesh=inner, in_specs=in_specs, out_specs=out_specs, check_vma=False)
```

profile of v0, /device:TPU:1, one launch (start us, length us, event | category | flops | bytes accessed | tf_op | source)
XLA Modules:
  0.0 255.3 jit_solution(2603240170650563449)
XLA Ops:
  8.0 0.0 copy-start
  8.0 0.0 all-gather.14.cloned.1.call-start
  8.1 23.0 %all-gather = bf16[64,1024]{1,0:T(8,128)(2,1)} all-gather(bf16[8,1024]{1,0:T(8,128)(2,1)} %param.20), channel_id=2, replica_groups=mesh['rz'=8,'ry'=8,'rc'=2,'grp'=4] {'ry'}, dimensions={0}, use_global_device_ids=true | all-gather | bytes 147456 | tf_op jit(solution)/shard_map/all_gather | solution.py:33
  31.0 0.0 all-gather.14.cloned.1.call-update
  31.1 0.0 all-gather.18.cloned.1.call-start
  31.1 27.1 %all-gather.3 = bf16[64,1024]{1,0:T(8,128)(2,1)} all-gather(bf16[8,1024]{1,0:T(8,128)(2,1)} %bitcast.90), channel_id=5, replica_groups=mesh['rz'=8,'ry'=8,'rc'=2,'grp'=4] {'rz'}, dimensions={0}, use_global_device_ids=true | all-gather | bytes 147456 | tf_op jit(solution)/shard_map/all_gather | solution.py:33
  58.2 0.0 all-gather.18.cloned.1.call-update
  58.2 0.0 reduce-scatter.3.cloned.1.call-start
  58.3 2.2 fusion.101
  60.5 0.0 copy-start.7
  60.5 0.1 convert_element_type.25
  60.6 0.1 slice_bitcast_fusion
  60.7 0.5 copy-done.7
  61.2 3.7 %while.11 = (s32[]{:T(128)}, bf16[4,512,64]{1,2,0:T(8,128)(2,1)S(1)}, bf16[4,512,64]{1,2,0:T(8,128)(2,1)S(1)}, bf16[4,512,64]{1,2,0:T(8,128)(2,1)S(1)}, bf16[4,5...) while((s32[]{:T(128)}, bf16[4,512,64]{1,2,0:T(8,128)(2,1)S(1)}, ...), condition=%wide.region_3.4_spmd.clone, body=%wide.region_0.3_spmd.clone.sunk | while | flops 70024192 | bytes 3424341 | solution.py:90
  61.2 0.4 fusion.113
  61.6 0.2 fusion.114
  61.8 0.3 fusion.115
  62.1 0.4 fusion.113
  62.5 0.2 fusion.114
  62.7 0.3 fusion.115
  63.1 0.4 fusion.113
  63.5 0.2 fusion.114
  63.7 0.3 fusion.115
  64.0 0.4 fusion.113
  64.4 0.2 fusion.114
  64.6 0.3 fusion.115
  64.9 2.8 %convolution_bitcast_fusion = f32[512,1024]{1,0:T(8,128)} fusion(bf16[4,64,1024]{2,1,0:T(8,128)(2,1)} %param.17, bf16[4,512,64]{1,2,0:T(8,128)(2,1)S(1)} %get-tuple-element.34), kind=kOutput, calls=%fused_computation.40 | convolution fusion | flops 268435456 | bytes 2883584 | tf_op jit(solution)/shard_map/nhd,hde->ne/dot_general | solution.py:93
  67.8 0.0 reduce-scatter.3.cloned.1.call-update
  67.8 0.0 all-gather.16.cloned.1.call-start
  67.9 10.0 %all-gather.14.cloned.1.call-done = bf16[64,8,1024]{2,1,0:T(8,128)(2,1)} async-done(((bf16[8,8,1024]{2,1,0:T(8,128)(2,1)}), bf16[64,8,1024]{2,1,0:T(8,128)(2,1)}) %all-gather.14.cloned.1.call-update) | async-done | bytes 1048592 | tf_op jit(solution)/shard_map/all_gather | solution.py:34
  77.9 0.0 all-gather.16.cloned.1.call-update
  78.0 0.0 all-gather.20.cloned.1.call-start
  78.0 41.6 %all-gather.18.cloned.1.call-done = bf16[64,8,1024]{2,1,0:T(8,128)(2,1)} async-done(((bf16[8,8,1024]{2,1,0:T(8,128)(2,1)}), bf16[64,8,1024]{2,1,0:T(8,128)(2,1)}) %all-gather.18.cloned.1.call-update) | async-done | bytes 1048592 | tf_op jit(solution)/shard_map/all_gather | solution.py:34
  119.6 0.0 all-gather.20.cloned.1.call-update
  119.6 0.0 all-gather.12.cloned.1.call-start
  119.7 0.0 reduce-scatter.3.cloned.1.call-done
  119.7 1.2 fusion.64
  120.9 1.2 multiply_reduce_fusion.1
  122.2 1.9 scatter_custom_fusion
  124.1 16.0 %all_to_all.10 = bf16[8,16,1024]{2,1,0:T(8,128)(2,1)S(1)} all-to-all(bf16[8,16,1024]{2,1,0:T(8,128)(2,1)S(1)} %bitcast.87), channel_id=1, replica_groups=mesh['rz'=8,'ry'=8,'rc'=2,'grp'=4] {'rz'}, dimensions={0} | all-to-all | bytes 524288 | tf_op jit(solution)/shard_map/all_to_all | solution.py:101
  140.1 0.1 copy.42
  140.3 21.8 %all_to_all.11 = bf16[8,16,1024]{2,0,1:T(8,128)(2,1)S(1)} all-to-all(bf16[8,16,1024]{2,0,1:T(8,128)(2,1)S(1)} %copy.42), channel_id=1, replica_groups=mesh['rz'=8,'ry'=8,'rc'=2,'grp'=4] {'ry','rc'}, dimensions={1} | all-to-all | bytes 524288 | tf_op jit(solution)/shard_map/all_to_all | solution.py:102
  162.1 0.9 copy.43
  162.9 0.0 all-gather.12.cloned.1.call-update
  162.9 0.2 reduce-scatter.5.cloned.1.call-start
  163.2 0.0 all-gather.16.cloned.1.call-done
  163.2 3.2 %copy.44 = bf16[8,8,2,8,1024]{4,3,2,1,0:T(8,128)(2,1)} copy(bf16[8,8,2,8,1024]{4,3,1,0,2:T(8,128)(2,1)} %bitcast.80) | data formatting | bytes 4194304 | tf_op jit(solution)/shard_map/transpose | solution.py:37
  166.4 0.1 all-gather.20.cloned.1.call-done
  166.5 3.1 %copy.45 = bf16[8,8,2,8,1024]{4,3,2,1,0:T(8,128)(2,1)} copy(bf16[8,8,2,8,1024]{4,3,0,1,2:T(8,128)(2,1)} %bitcast.81) | data formatting | bytes 4194304 | tf_op jit(solution)/shard_map/transpose | solution.py:39
  169.6 26.6 %all-gather.12.cloned.1.call-done = bf16[512,1024]{1,0:T(8,128)(2,1)} async-done(((bf16[128,1024]{1,0:T(8,128)(2,1)}), bf16[512,1024]{1,0:T(8,128)(2,1)}) %all-gather.12.cloned.1.call-update) | async-done | bytes 1048592 | tf_op jit(solution)/shard_map/all_gather | solution.py:104
  196.3 10.1 %fusion.25 = f32[512,1024]{1,0:T(8,128)} fusion(bf16[1024,1024]{1,0:T(8,128)(2,1)} %bitcast.83, bf16[512,1024]{1,0:T(8,128)(2,1)} %all-gather.12.cloned.1.call-done, bf16[1024,1024]{1,0:T(8,128)(2,1)} %bitcast.82), kind=kOutput, calls=%fused_computation.41 | convolution fusion | flops 2181562368 | bytes 7340032 | tf_op jit(solution)/shard_map/dot_general | solution.py:107
  206.4 0.0 reduce-scatter.5.cloned.1.call-update
  206.5 0.1 reshape.123
  206.6 0.0 copy-start.1
  206.6 0.4 copy.46
  207.0 0.1 copy-done.9
  207.1 0.1 broadcast_in_dim.18
  207.2 0.0 copy-start.5
  207.2 0.8 scatter_fusion
  208.0 1.2 copy.47
  209.2 34.7 %reduce-scatter.5.cloned.1.call-done = f32[128,1024]{1,0:T(8,128)} async-done(((f32[512,1024]{1,0:T(8,128)}), f32[128,1024]{1,0:T(8,128)}) %reduce-scatter.5.cloned.1.call-update) | async-done | bytes 524304 | tf_op jit(solution)/shard_map/reduce_scatter | solution.py:110
  243.9 1.2 fusion.63
  245.0 1.2 multiply_reduce_fusion
  246.3 1.9 add_convert_fusion
  (22 shorter events, 0.1 us)
Async XLA Ops:
  8.0 50.3 %copy-start = (bf16[1024,4,192]{0,2,1:T(8,128)(2,1)S(1)}, bf16[1024,4,192]{0,2,1:T(8,128)(2,1)}, u32[]{:S(2)}) copy-start(bf16[1024,4,192]{0,2,1:T(8,128)(2,1)} %param.16) | copy-start | bytes 4718596
  8.0 69.9 %all-gather.14.cloned.1.call-start = ((), (), s32[]{:S(2)}) async-start(), calls=%async_computation.7 | async-start | bytes 1179648 | tf_op jit(solution)/shard_map/all_gather | solution.py:34
  31.1 88.5 %all-gather.18.cloned.1.call-start = ((), (), s32[]{:S(2)}) async-start(), calls=%async_computation.9 | async-start | bytes 1179648 | tf_op jit(solution)/shard_map/all_gather | solution.py:34
  58.2 61.5 %reduce-scatter.3.cloned.1.call-start = ((), (), s32[]{:S(2)}) async-start(), calls=%async_computation.4 | async-start | bytes 2621440 | tf_op jit(solution)/shard_map/reduce_scatter | solution.py:96
  60.5 0.7 copy-start.7
  67.8 51.9 %copy-start.8 = (s32[1,1,128]{2,1,0:T(1,128)S(1)}, s32[1,1,128]{2,1,0:T(1,128)}, u32[]{:S(2)}) copy-start(s32[1,1,128]{2,1,0:T(1,128)} %param.25) | copy-start | bytes 1540
  67.8 51.9 %copy-start.2 = (bf16[512,1024]{1,0:T(8,128)(2,1)S(1)}, bf16[512,1024]{1,0:T(8,128)(2,1)}, u32[]{:S(2)}) copy-start(bf16[512,1024]{1,0:T(8,128)(2,1)} %param.14) | copy-start | bytes 3145732
  67.8 54.4 %copy-start.3 = (f32[1024]{0:T(1024)S(1)}, f32[1024]{0:T(1024)}, u32[]{:S(2)}) copy-start(f32[1024]{0:T(1024)} %param.19) | copy-start | bytes 12292
  67.8 54.4 %copy-start.4 = (f32[1024]{0:T(1024)S(1)}, f32[1024]{0:T(1024)}, u32[]{:S(2)}) copy-start(f32[1024]{0:T(1024)} %param.18) | copy-start | bytes 12292
  67.8 95.4 %all-gather.16.cloned.1.call-start = ((), (), s32[]{:S(2)}) async-start(), calls=%async_computation.8 | async-start | bytes 3145728 | tf_op jit(solution)/shard_map/all_gather | solution.py:35
  78.0 88.5 %all-gather.20.cloned.1.call-start = ((), (), s32[]{:S(2)}) async-start(), calls=%async_computation.10 | async-start | bytes 3145728 | tf_op jit(solution)/shard_map/all_gather | solution.py:35
  119.6 76.6 %all-gather.12.cloned.1.call-start = ((), (), s32[]{:S(2)}) async-start(), calls=%async_computation.5 | async-start | bytes 1310720 | tf_op jit(solution)/shard_map/all_gather | solution.py:104
  162.9 80.9 %reduce-scatter.5.cloned.1.call-start = ((), (), s32[]{:S(2)}) async-start(), calls=%async_computation.6 | async-start | bytes 2621440 | tf_op jit(solution)/shard_map/reduce_scatter | solution.py:110
  206.4 0.7 copy-start.9
  206.6 37.3 %copy-start.1 = (bf16[8,16,1024]{2,1,0:T(8,128)(2,1)S(1)}, bf16[8,16,1024]{2,1,0:T(8,128)(2,1)}, u32[]{:S(2)}) copy-start(bf16[8,16,1024]{2,1,0:T(8,128)(2,1)} %copy.43) | copy-start | bytes 786436
  207.2 39.1 %copy-start.5 = (f32[1024]{0:T(1024)S(1)}, f32[1024]{0:T(1024)}, u32[]{:S(2)}) copy-start(f32[1024]{0:T(1024)} %param.23) | copy-start | bytes 12292
  207.2 39.1 %copy-start.6 = (f32[1024]{0:T(1024)S(1)}, f32[1024]{0:T(1024)}, u32[]{:S(2)}) copy-start(f32[1024]{0:T(1024)} %param.22) | copy-start | bytes 12292
Sparse Core Ops, SparseCore 0:
  31.2 46.7 all-gather.13
  80.0 39.5 all-gather.17
  121.7 22.7 all-gather.15
  146.4 20.0 all-gather.19
  169.0 27.1 all-gather.11
Sparse Core Ops, SparseCore 1:
  67.9 44.0 reduce-scatter.2
  206.5 37.3 reduce-scatter.4
where the time goes:
time: 256 us; the launch traced here: 255 us
  waiting for transfers between devices  113 us (44%)
  blocking collectives  87.8 us (34%)
  matrix products  18.1 us (7%)
  between operations  15.5 us (6%)
  local copies, waits for them, and re-layouts  10.6 us (4%)
  other arithmetic  9.59 us (4%)
    all_gather x2, waiting for transfers between devices, gather_rows(): b = lax.all_gather(a, second, axis=0, tiled=False)  51.6 us
    all_gather x2, blocking collectives, gather_rows(): a = lax.all_gather(block, first, axis=0, tiled=False)  50 us
    reduce_scatter x1, waiting for transfers between devices, local(): lax.psum_scatter(lowered_all, 'grp', scatter_dimension=0, tiled=True)  34.7 us
    all_gather x1, waiting for transfers between devices, local(): group_rows = lax.all_gather(even_rows, 'grp', axis=0, tiled=True)  26.6 us
    all_to_all x1, blocking collectives, local(): lax.all_to_all(staged, ('ry', 'rc'), split_axis=1, concat_axis=1, tiled=T...  21.8 us
    all_to_all x1, blocking collectives, local(): lax.all_to_all(staged, 'rz', split_axis=0, concat_axis=0, tiled=True)  16 us
    dot_general x1, matrix products, local(): lax.dot_general(activated, down_full_t, (((1,), (1,)), ((), ())), preferr...  10.1 us
  transfers between devices with their start and end apart: 7, of which 5 were waited for; matrix products, arithmetic and copies ran while one was open for 9% of the time, Pallas kernels for 0%

commit v1 on v0

--- a/solution.py
+++ b/solution.py
@@ -101,7 +101,9 @@
     staged = lax.all_to_all(staged, "rz", split_axis=0, concat_axis=0, tiled=True)
     staged = lax.all_to_all(staged, ("ry", "rc"), split_axis=1, concat_axis=1, tiled=True)
     even_rows = staged.reshape(quarter, width)
-    group_rows = lax.all_gather(even_rows, "grp", axis=0, tiled=True)
+    group_rows = jnp.concatenate(
+        lax.all_to_all(jnp.stack([even_rows] * lax.axis_size("grp")), "grp", 0, 0), axis=0
+    )
     raised = jnp.dot(group_rows, up_full, preferred_element_type=jnp.float32)
     activated = jax.nn.gelu(raised, approximate=False).astype(jnp.bfloat16)
     lowered_all = lax.dot_general(

time: 256 us -> 230 us (0.90)
  waiting for transfers between devices: 113 us -> 82.6 us
  starting transfers between devices: 0.46 us -> 4.69 us
    all_gather x1 -> x0, waiting for transfers between devices: 26.6 us -> none  [local(): group_rows = lax.all_gather(even_rows, 'grp', axis=0, tiled=True)]
    reduce_scatter x1, waiting for transfers between devices: 34.7 us -> 21.9 us  [local(): lax.psum_scatter(lowered_all, 'grp', scatter_dimension=0, tiled=True)]
    all_to_all x0 -> x1, waiting for transfers between devices: none -> 9.02 us  [local(): lax.all_to_all(jnp.stack([even_rows] * lax.axis_size('grp')), 'grp', 0, 0)]
    all_to_all x0 -> x1, starting transfers between devices: none -> 4.26 us  [local(): lax.all_to_all(jnp.stack([even_rows] * lax.axis_size('grp')), 'grp', 0, 0)]
  transfers between devices with their start and end apart: 7 -> 7, of which waited for: 5 -> 4; matrix products, arithmetic and copies ran while one was open for 9% -> 10% of each run, Pallas kernels for 0% -> 0%
where the time goes in v1:
time: 230 us; the launch traced here: 229 us
  blocking collectives  87.8 us (38%)
  waiting for transfers between devices  82.6 us (36%)
  matrix products  18.1 us (8%)
  between operations  15.5 us (7%)
  local copies, waits for them, and re-layouts  11 us (5%)
  other arithmetic  9.59 us (4%)
  starting transfers between devices  4.69 us (2%)
    all_gather x2, waiting for transfers between devices, gather_rows(): b = lax.all_gather(a, second, axis=0, tiled=False)  51.6 us
    all_gather x2, blocking collectives, gather_rows(): a = lax.all_gather(block, first, axis=0, tiled=False)  50 us
    reduce_scatter x1, waiting for transfers between devices, local(): lax.psum_scatter(lowered_all, 'grp', scatter_dimension=0, tiled=True)  21.9 us
    all_to_all x1, blocking collectives, local(): lax.all_to_all(staged, ('ry', 'rc'), split_axis=1, concat_axis=1, tiled=T...  21.8 us
    all_to_all x1, blocking collectives, local(): lax.all_to_all(staged, 'rz', split_axis=0, concat_axis=0, tiled=True)  16 us
    dot_general x1, matrix products, local(): lax.dot_general(activated, down_full_t, (((1,), (1,)), ((), ())), preferr...  10.1 us
    all_to_all x1, waiting for transfers between devices, local(): lax.all_to_all(jnp.stack([even_rows] * lax.axis_size('grp')), 'grp', 0, 0)  9.02 us
  transfers between devices with their start and end apart: 7, of which 4 were waited for; matrix products, arithmetic and copies ran while one was open for 10% of the time, Pallas kernels for 0%

profile of v1, /device:TPU:1, one launch (start us, length us, event | category | flops | bytes accessed | tf_op | source)
XLA Modules:
  0.0 229.3 jit_solution(2332186780631335022)
XLA Ops:
  8.0 0.0 copy-start
  8.0 0.0 all-gather.11.cloned.1.call-start
  8.1 23.0 %all-gather = bf16[64,1024]{1,0:T(8,128)(2,1)} all-gather(bf16[8,1024]{1,0:T(8,128)(2,1)} %param.20), channel_id=2, replica_groups=mesh['rz'=8,'ry'=8,'rc'=2,'grp'=4] {'ry'}, dimensions={0}, use_global_device_ids=true | all-gather | bytes 147456 | tf_op jit(solution)/shard_map/all_gather | solution.py:33
  31.0 0.0 all-gather.11.cloned.1.call-update
  31.1 0.0 all-gather.15.cloned.1.call-start
  31.1 27.1 %all-gather.3 = bf16[64,1024]{1,0:T(8,128)(2,1)} all-gather(bf16[8,1024]{1,0:T(8,128)(2,1)} %bitcast.91), channel_id=5, replica_groups=mesh['rz'=8,'ry'=8,'rc'=2,'grp'=4] {'rz'}, dimensions={0}, use_global_device_ids=true | all-gather | bytes 147456 | tf_op jit(solution)/shard_map/all_gather | solution.py:33
  58.2 0.0 all-gather.15.cloned.1.call-update
  58.2 0.0 reduce-scatter.3.cloned.1.call-start
  58.3 2.2 fusion.101
  60.5 0.0 copy-start.6
  60.5 0.1 convert_element_type.25
  60.6 0.1 slice_bitcast_fusion
  60.7 0.5 copy-done.6
  61.2 3.7 %while.11 = (s32[]{:T(128)}, bf16[4,512,64]{1,2,0:T(8,128)(2,1)S(1)}, bf16[4,512,64]{1,2,0:T(8,128)(2,1)S(1)}, bf16[4,512,64]{1,2,0:T(8,128)(2,1)S(1)}, bf16[4,5...) while((s32[]{:T(128)}, bf16[4,512,64]{1,2,0:T(8,128)(2,1)S(1)}, ...), condition=%wide.region_3.4_spmd.clone, body=%wide.region_0.3_spmd.clone.sunk | while | flops 70024192 | bytes 3424341 | solution.py:90
  61.2 0.4 fusion.113
  61.6 0.2 fusion.114
  61.8 0.3 fusion.115
  62.1 0.4 fusion.113
  62.5 0.2 fusion.114
  62.7 0.3 fusion.115
  63.1 0.4 fusion.113
  63.5 0.2 fusion.114
  63.7 0.3 fusion.115
  64.0 0.4 fusion.113
  64.4 0.2 fusion.114
  64.6 0.3 fusion.115
  64.9 2.9 %convolution_bitcast_fusion = f32[512,1024]{1,0:T(8,128)} fusion(bf16[4,64,1024]{2,1,0:T(8,128)(2,1)} %param.17, bf16[4,512,64]{1,2,0:T(8,128)(2,1)S(1)} %get-tuple-element.34), kind=kOutput, calls=%fused_computation.40 | convolution fusion | flops 268435456 | bytes 2883584 | tf_op jit(solution)/shard_map/nhd,hde->ne/dot_general | solution.py:93
  67.8 0.0 reduce-scatter.3.cloned.1.call-update
  67.8 0.0 copy-start.2
  67.8 0.0 copy-start.3
  67.8 0.0 all-gather.13.cloned.1.call-start
  67.9 10.0 %all-gather.11.cloned.1.call-done = bf16[64,8,1024]{2,1,0:T(8,128)(2,1)} async-done(((bf16[8,8,1024]{2,1,0:T(8,128)(2,1)}), bf16[64,8,1024]{2,1,0:T(8,128)(2,1)}) %all-gather.11.cloned.1.call-update) | async-done | bytes 1048592 | tf_op jit(solution)/shard_map/all_gather | solution.py:34
  77.9 0.0 all-gather.13.cloned.1.call-update
  78.0 0.0 all-gather.17.cloned.1.call-start
  78.0 41.6 %all-gather.15.cloned.1.call-done = bf16[64,8,1024]{2,1,0:T(8,128)(2,1)} async-done(((bf16[8,8,1024]{2,1,0:T(8,128)(2,1)}), bf16[64,8,1024]{2,1,0:T(8,128)(2,1)}) %all-gather.15.cloned.1.call-update) | async-done | bytes 1048592 | tf_op jit(solution)/shard_map/all_gather | solution.py:34
  119.6 0.0 all-gather.17.cloned.1.call-update
  119.6 0.0 reduce-scatter.3.cloned.1.call-done
  119.7 1.2 fusion.64
  120.9 1.2 multiply_reduce_fusion.1
  122.1 1.9 scatter_custom_fusion
  124.0 16.0 %all_to_all.15 = bf16[8,16,1024]{2,1,0:T(8,128)(2,1)S(1)} all-to-all(bf16[8,16,1024]{2,1,0:T(8,128)(2,1)S(1)} %bitcast.88), channel_id=1, replica_groups=mesh['rz'=8,'ry'=8,'rc'=2,'grp'=4] {'rz'}, dimensions={0} | all-to-all | bytes 524288 | tf_op jit(solution)/shard_map/all_to_all | solution.py:101
  140.1 0.1 copy.42
  140.2 21.8 %all_to_all.16 = bf16[8,16,1024]{2,0,1:T(8,128)(2,1)S(1)} all-to-all(bf16[8,16,1024]{2,0,1:T(8,128)(2,1)S(1)} %copy.42), channel_id=1, replica_groups=mesh['rz'=8,'ry'=8,'rc'=2,'grp'=4] {'ry','rc'}, dimensions={1} | all-to-all | bytes 524288 | tf_op jit(solution)/shard_map/all_to_all | solution.py:102
  162.0 0.1 copy.43
  162.1 1.1 stack.3
  163.2 4.3 %all-to-all-start.2 = ((bf16[4,128,1024]{2,1,0:T(8,128)(2,1)}), bf16[4,128,1024]{2,1,0:T(8,128)(2,1)}, u32[]{:S(2)}, u32[]{:S(2)}) async-start(bf16[4,128,1024]{2,1,0:T(8,128)(2,1)} %stack.3), calls=%async_computation.3 | async-start | bytes 2097152 | tf_op jit(solution)/shard_map/all_to_all | solution.py:105
  167.5 0.2 reduce-scatter.5.cloned.1.call-start
  167.7 0.0 all-gather.13.cloned.1.call-done
  167.8 3.2 %copy.44 = bf16[8,8,2,8,1024]{4,3,2,1,0:T(8,128)(2,1)} copy(bf16[8,8,2,8,1024]{4,3,1,0,2:T(8,128)(2,1)} %bitcast.81) | data formatting | bytes 4194304 | tf_op jit(solution)/shard_map/transpose | solution.py:37
  170.9 3.1 %copy.45 = bf16[8,8,2,8,1024]{4,3,2,1,0:T(8,128)(2,1)} copy(bf16[8,8,2,8,1024]{4,3,0,1,2:T(8,128)(2,1)} %bitcast.82) | data formatting | bytes 4194304 | tf_op jit(solution)/shard_map/transpose | solution.py:39
  174.1 9.0 %all-to-all-done.2 = bf16[4,128,1024]{2,1,0:T(8,128)(2,1)} async-done(((bf16[4,128,1024]{2,1,0:T(8,128)(2,1)}), bf16[4,128,1024]{2,1,0:T(8,128)(2,1)}, u32[]{:S(2)}, u32[]{:S(2)}) %all-to-all-start.2) | async-done | bytes 1048608 | tf_op jit(solution)/shard_map/all_to_all | solution.py:105
  183.1 10.1 %fusion.25 = f32[512,1024]{1,0:T(8,128)} fusion(bf16[1024,1024]{1,0:T(8,128)(2,1)} %bitcast.84, bf16[512,1024]{1,0:T(8,128)(2,1)} %bitcast.12, bf16[1024,1024]{1,0:T(8,128)(2,1)} %bitcast.83), kind=kOutput, calls=%fused_computation.41 | convolution fusion | flops 2181562368 | bytes 7340032 | tf_op jit(solution)/shard_map/dot_general | solution.py:109
  193.2 0.0 reduce-scatter.5.cloned.1.call-update
  193.2 0.0 copy-start.8
  193.3 0.1 reshape.129
  193.4 0.4 copy.46
  193.8 0.1 copy-done.8
  193.9 0.1 broadcast_in_dim.18
  194.0 0.8 scatter_fusion
  194.8 1.2 copy.47
  196.0 21.9 %reduce-scatter.5.cloned.1.call-done = f32[128,1024]{1,0:T(8,128)} async-done(((f32[512,1024]{1,0:T(8,128)}), f32[128,1024]{1,0:T(8,128)}) %reduce-scatter.5.cloned.1.call-update) | async-done | bytes 524304 | tf_op jit(solution)/shard_map/reduce_scatter | solution.py:112
  217.8 1.2 fusion.63
  219.0 1.2 multiply_reduce_fusion
  220.3 1.9 add_convert_fusion
  (20 shorter events, 0.1 us)
Async XLA Ops:
  8.0 50.3 %copy-start = (bf16[1024,4,192]{0,2,1:T(8,128)(2,1)S(1)}, bf16[1024,4,192]{0,2,1:T(8,128)(2,1)}, u32[]{:S(2)}) copy-start(bf16[1024,4,192]{0,2,1:T(8,128)(2,1)} %param.16) | copy-start | bytes 4718596
  8.0 69.9 %all-gather.11.cloned.1.call-start = ((), (), s32[]{:S(2)}) async-start(), calls=%async_computation.7 | async-start | bytes 1179648 | tf_op jit(solution)/shard_map/all_gather | solution.py:34
  31.1 88.5 %all-gather.15.cloned.1.call-start = ((), (), s32[]{:S(2)}) async-start(), calls=%async_computation.9 | async-start | bytes 1179648 | tf_op jit(solution)/shard_map/all_gather | solution.py:34
  58.2 61.5 %reduce-scatter.3.cloned.1.call-start = ((), (), s32[]{:S(2)}) async-start(), calls=%async_computation.5 | async-start | bytes 2621440 | tf_op jit(solution)/shard_map/reduce_scatter | solution.py:96
  60.5 0.7 copy-start.6
  67.8 10.2 %copy-start.7 = (s32[1,1,128]{2,1,0:T(1,128)S(1)}, s32[1,1,128]{2,1,0:T(1,128)}, u32[]{:S(2)}) copy-start(s32[1,1,128]{2,1,0:T(1,128)} %param.25) | copy-start | bytes 1540
  67.8 51.9 %copy-start.1 = (bf16[512,1024]{1,0:T(8,128)(2,1)S(1)}, bf16[512,1024]{1,0:T(8,128)(2,1)}, u32[]{:S(2)}) copy-start(bf16[512,1024]{1,0:T(8,128)(2,1)} %param.14) | copy-start | bytes 3145732
  67.8 54.3 %copy-start.2 = (f32[1024]{0:T(1024)S(1)}, f32[1024]{0:T(1024)}, u32[]{:S(2)}) copy-start(f32[1024]{0:T(1024)} %param.19) | copy-start | bytes 12292
  67.8 54.3 %copy-start.3 = (f32[1024]{0:T(1024)S(1)}, f32[1024]{0:T(1024)}, u32[]{:S(2)}) copy-start(f32[1024]{0:T(1024)} %param.18) | copy-start | bytes 12292
  67.8 99.9 %all-gather.13.cloned.1.call-start = ((), (), s32[]{:S(2)}) async-start(), calls=%async_computation.8 | async-start | bytes 3145728 | tf_op jit(solution)/shard_map/all_gather | solution.py:35
  78.0 93.0 %all-gather.17.cloned.1.call-start = ((), (), s32[]{:S(2)}) async-start(), calls=%async_computation.10 | async-start | bytes 3145728 | tf_op jit(solution)/shard_map/all_gather | solution.py:35
  163.2 19.9 %all-to-all-start.2 = ((bf16[4,128,1024]{2,1,0:T(8,128)(2,1)}), bf16[4,128,1024]{2,1,0:T(8,128)(2,1)}, u32[]{:S(2)}, u32[]{:S(2)}) async-start(bf16[4,128,1024]{2,1,0:T(8,128)(2,1)} %stack.3), calls=%async_computation.3 | async-start | bytes 2097152 | tf_op jit(solution)/shard_map/all_to_all | solution.py:105
  167.5 50.3 %reduce-scatter.5.cloned.1.call-start = ((), (), s32[]{:S(2)}) async-start(), calls=%async_computation.6 | async-start | bytes 2621440 | tf_op jit(solution)/shard_map/reduce_scatter | solution.py:112
  193.2 0.7 copy-start.8
  194.0 26.3 %copy-start.4 = (f32[1024]{0:T(1024)S(1)}, f32[1024]{0:T(1024)}, u32[]{:S(2)}) copy-start(f32[1024]{0:T(1024)} %param.23) | copy-start | bytes 12292
  194.0 26.3 %copy-start.5 = (f32[1024]{0:T(1024)S(1)}, f32[1024]{0:T(1024)}, u32[]{:S(2)}) copy-start(f32[1024]{0:T(1024)} %param.22) | copy-start | bytes 12292
Sparse Core Ops, SparseCore 0:
  31.2 46.7 all-gather.10
  80.0 39.5 all-gather.14
  121.7 22.7 all-gather.12
  146.4 20.0 all-gather.16
Sparse Core Ops, SparseCore 1:
  67.9 44.0 reduce-scatter.2
  193.3 24.5 reduce-scatter.4
